TPU v7x, 128 devices: a whole 4x4x4 slice. The times are simulated.
128 devices in a mesh: fsdp: 32 (over z, y, core), fac: 4 (over x).
Axes of the slice: x: 4, y: 4, z: 4, core: 2. Of those that a mesh axis runs over, the one named last changes fastest.
Arguments:
- activations: bfloat16 [32768, 3072], P('fsdp'), may hold values from -6 to 6
- out_grads: bfloat16 [32768, 3072], P('fsdp', 'fac'), may hold values from -12 to 12
- token_ids: int32 [32768], P('fsdp'), may hold values from 0 to 32767
- forget_mask: int32 [32768], P('fsdp'), may hold values 0 or 1
- importance: float32 [32768], replicated, may hold values from 0.3 to 3
- in_inverse: bfloat16 [3072, 3072], P('fsdp'), may hold values from -1 to 3, as said below
- out_inverse: bfloat16 [3072, 3072], P(None, 'fac'), may hold values from -1 to 3, as said below
Outputs:
- newton_step: float32 [3072, 3072], P('fsdp', 'fac')
- residual: float32 [3072, 3072], P('fsdp', 'fac')
Inputs may be any that keep to these rules, and one draw needn't show every extreme that they name: `in_inverse`: symmetric and positive definite. `out_inverse`: symmetric and positive definite.
All inputs are finite; a program needn't handle non-finite values. No bound on the sum of `forget_mask` on one device may be relied on, other than what follows from the above.
Results may differ from a plain program's by a relative error of at most 0.03.
Values may be sent and summed in bfloat16 or wider, within the bound.
No kernel may reach another device: no remote copies, remote signals or barrier semaphores. Data moves between devices by JAX's collectives and lax.ppermute only.
A program may use at most 64 MiB of HBM per device.

v0:
```python
import math
import jax
import jax.numpy as jnp
from jax import lax
from jax.sharding import PartitionSpec as P

ITERS = 2
damping = 0.3


def add_columns(matrix, piece):
    return jnp.dot(matrix, piece, preferred_element_type=jnp.float32)


def transposed_term(matrix, right):
    return lax.dot_general(
        matrix, right, (((0,), (0,)), ((), ())), preferred_element_type=jnp.float32
    )


FSDP = ("pairs", "core")


def ring_product(piece, right):
    n = lax.axis_size("fac")
    me = lax.axis_index("fac")
    width = piece.shape[1]

    def right_block(k):
        return lax.dynamic_slice_in_dim(right, k % n * width, width, axis=0)

    total = add_columns(piece, right_block(me))
    ahead = piece
    behind = piece
    for step in range(1, n // 2 + 1):
        ahead = lax.ppermute(ahead, "fac", [(j, (j + 1) % n) for j in range(n)])
        total = total + add_columns(ahead, right_block(me - step))
        if 2 * step < n:
            behind = lax.ppermute(behind, "fac", [(j, (j - 1) % n) for j in range(n)])
            total = total + add_columns(behind, right_block(me + step))
    return total


def scatter_sum(partial):
    pairs, cores = (lax.axis_size("pairs"), lax.axis_size("core"))
    blocks = partial.reshape(pairs, cores, partial.shape[0] // (pairs * cores), partial.shape[1])
    on_chip = lax.all_to_all(blocks, "core", 1, 1, tiled=False)
    chip_sum = jnp.sum(on_chip.astype(jnp.float32), axis=1).astype(jnp.bfloat16)
    received = lax.all_to_all(chip_sum, "pairs", 0, 0, tiled=False)
    return lax.optimization_barrier(jnp.sum(received.astype(jnp.float32), axis=0))


def global_sums(*partials):
    devices = lax.axis_size("pairs") * lax.axis_size("core") * lax.axis_size("fac")
    stacked = jnp.broadcast_to(jnp.stack(partials)[None, :], (devices, len(partials)))
    received = lax.all_to_all(stacked, FSDP + ("fac",), 0, 0, tiled=True)
    total = jnp.sum(received, axis=0)
    return tuple((total[i] for i in range(len(partials))))


def body(activations, out_grads, token_ids, forget_mask, importance, in_inverse, out_inverse):
    tok_rows, d_in = activations.shape
    total = tok_rows * lax.axis_size("pairs") * lax.axis_size("core")
    keep = 1.0 - forget_mask.astype(jnp.float32)
    weights = importance[token_ids] * keep / total
    forget_grads = out_grads * forget_mask.astype(jnp.bfloat16)[:, None]
    grad_scale = 1.0 / math.sqrt(total)
    gradient = scatter_sum(
        (transposed_term(activations, forget_grads) * grad_scale).astype(jnp.bfloat16)
    )

    def gather_rows(matrix):
        return lax.all_gather(matrix.astype(jnp.bfloat16), FSDP, axis=0, tiled=True)

    def precondition(gathered):
        mixed = add_columns(in_inverse, gathered)
        mixed_low = mixed.astype(jnp.bfloat16)
        return jnp.dot(
            lax.all_gather(mixed_low, "fac", axis=1, tiled=True),
            out_inverse,
            preferred_element_type=jnp.float32,
        )

    def inner_part(left, right):
        return jnp.sum(left * right)

    d_out_part = out_inverse.shape[1]
    in_cols = lax.all_gather(
        lax.dynamic_slice_in_dim(
            in_inverse, lax.axis_index("fac") * d_out_part, d_out_part, axis=1
        ),
        FSDP,
        axis=0,
        tiled=True,
    )
    gradient, in_cols = lax.optimization_barrier((gradient, in_cols))
    residual = -gradient
    residual_rows = gather_rows(residual)
    gram_cols = d_in // lax.axis_size("fac")
    own_cols = lax.dynamic_slice_in_dim(
        activations, lax.axis_index("fac") * gram_cols, gram_cols, axis=1
    )
    weighted = (own_cols * weights[:, None]).astype(jnp.bfloat16)
    half = gram_cols // 2
    gram_first = transposed_term(activations, weighted[:, :half]).astype(jnp.bfloat16)
    gram_second = transposed_term(activations, weighted[:, half:]).astype(jnp.bfloat16)
    residual_rows, first_rows = lax.optimization_barrier((residual_rows, scatter_sum(gram_first)))
    precond = precondition(residual_rows)
    gram_own = jnp.concatenate([first_rows, scatter_sum(gram_second)], axis=1)
    gram_rows = lax.all_gather(gram_own.astype(jnp.bfloat16), "fac", axis=1, tiled=True)

    def curvature(matrix):
        return add_columns(gram_rows, gather_rows(matrix)) + damping * matrix

    direction = precond
    image = curvature(direction)
    image_rows = gather_rows(image)
    inner_now, energy = global_sums(inner_part(residual, precond), inner_part(direction, image))
    gram_inverse = lax.all_gather(
        add_columns(gram_rows, in_cols).astype(jnp.bfloat16), "fac", axis=1, tiled=True
    )
    alpha = inner_now / energy
    newton_step = alpha * direction
    residual = residual - alpha * image
    next_rows = (residual_rows.astype(jnp.float32) - alpha * image_rows.astype(jnp.float32)).astype(
        jnp.bfloat16
    )
    rows = in_inverse.shape[0]
    left = jnp.concatenate([in_inverse, gram_inverse], axis=0)
    both = add_columns(left, next_rows).astype(jnp.bfloat16)
    both_out = ring_product(both, out_inverse)
    precond = both_out[:rows]
    precond_image = both_out[rows:] + damping * precond
    inner_next, z_hz, z_hd, d_hz = global_sums(
        inner_part(residual, precond),
        inner_part(precond, precond_image),
        inner_part(precond, image),
        inner_part(direction, precond_image),
    )
    beta = inner_next / inner_now
    direction = precond + beta * direction
    image = precond_image + beta * image
    energy = z_hz + beta * (z_hd + d_hz) + beta * beta * energy
    alpha = inner_next / energy
    newton_step = newton_step + alpha * direction
    residual = residual - alpha * image
    return (newton_step, residual)


def solution(mesh):
    cores = 2
    split = jax.sharding.Mesh(
        mesh.devices.reshape(mesh.shape["fsdp"] // cores, cores, mesh.shape["fac"]),
        ("pairs", "core", "fac"),
    )
    placed = (P(FSDP, None), P(FSDP, "fac"), P(FSDP), P(FSDP), P(), P(FSDP, None), P(None, "fac"))
    return jax.shard_map(
        body,
        mesh=split,
        in_specs=placed,
        out_specs=(P(FSDP, "fac"), P(FSDP, "fac")),
        check_vma=False,
    )
```

profile of v0, /device:TPU:1, one launch (start us, length us, event | category | flops | bytes accessed | tf_op | source)
XLA Modules:
  0.0 333.9 jit_solution(15328082240654221681)
XLA Ops:
  7.2 0.0 all-gather.5.cloned.1.call-start
  7.2 1.6 constant_dynamic-slice_fusion
  8.8 0.0 all-gather.5.cloned.1.call-update
  8.8 0.0 all-gather.7.cloned.1.call-start
  8.9 0.7 convert_element_type.76
  9.6 9.4 %fusion.2 = bf16[3072,768]{0,1:T(8,128)(2,1)} fusion(bf16[1024,3072]{1,0:T(8,128)(2,1)} %param.7, bf16[1024,768]{1,0:T(8,128)(2,1)} %param.8, bf16[1024]{0:T(1024)(128)(2,1)S(1)} %convert_element_type.76), kind=kOutput, calls=%fused_computation.6 | convolution fusion | flops 4837343232 | bytes 12584960 | tf_op jit(solution)/shard_map/dot_general | solution.py:16
  19.0 6.7 %copy.24 = bf16[3072,768]{1,0:T(8,128)(2,1)} copy(bf16[3072,768]{0,1:T(8,128)(2,1)} %fusion.2) | data formatting | bytes 9437184 | tf_op jit(solution)/shard_map/convert_element_type | solution.py:69
  25.6 2.7 copy.25
  28.3 9.7 %all_to_all.42 = bf16[16,2,96,768]{3,2,0,1:T(8,128)(2,1)} all-to-all(bf16[16,2,96,768]{3,2,0,1:T(8,128)(2,1)S(1)} %copy.25), channel_id=1, replica_groups=mesh['pairs'=16,'core'=2,'fac'=4] {'core'}, dimensions={1} | all-to-all | bytes 9437184 | tf_op jit(solution)/shard_map/all_to_all | solution.py:47
  38.0 3.5 %reduce_sum.135 = bf16[16,96,768]{2,1,0:T(8,128)(2,1)S(1)} reduce(bf16[16,2,96,768]{3,2,0,1:T(8,128)(2,1)} %all_to_all.42, bf16[]{:T(256)} %constant.44.clone.1), dimensions={1}, to_apply=%region_0.0 | reduce | flops 1179648 | bytes 7077890 | tf_op jit(solution)/shard_map/reduce_sum | solution.py:48
  41.5 43.2 %all_to_all.43 = bf16[16,96,768]{2,1,0:T(8,128)(2,1)S(1)} all-to-all(bf16[16,96,768]{2,1,0:T(8,128)(2,1)S(1)} %reduce_sum.135), channel_id=1, replica_groups=mesh['pairs'=16,'core'=2,'fac'=4] {'pairs'}, dimensions={0} | all-to-all | bytes 4718592 | tf_op jit(solution)/shard_map/all_to_all | solution.py:49
  84.7 0.3 convert_reduce_fusion
  85.1 0.0 all-gather.5.cloned.1.call-done
  85.1 0.7 negate_convert_fusion
  85.8 0.0 all-gather.7.cloned.1.call-update
  85.8 0.0 all-gather.9.cloned.1.call-start
  85.9 6.2 %gather_fusion = f32[1024]{0:T(1024)S(1)} fusion(f32[32768]{0:T(1024)S(1)} %copy-done, s32[1024]{0:T(1024)S(1)} %fusion.19), kind=kCustom, calls=%fused_computation | custom fusion | bytes 12288 | tf_op jit(solution)/shard_map/gather | solution.py:65
  92.1 1.7 multiply_convert_fusion.1
  93.8 1.1 copy-done.2
  95.0 7.0 %fusion.3 = bf16[3072,384]{0,1:T(8,128)(2,1)} fusion(bf16[1024,3072]{1,0:T(8,128)(2,1)} %param.7, bf16[1024,768]{1,0:T(8,128)(2,1)S(1)} %multiply_convert_fusion.1), kind=kOutput, calls=%fused_computation.9 | convolution fusion | flops 2417098752 | bytes 9437184 | tf_op jit(solution)/shard_map/dot_general | solution.py:16
  101.9 3.0 copy.26
  104.9 0.2 copy.27
  105.2 6.1 %all_to_all.44 = bf16[16,2,96,384]{3,2,0,1:T(8,128)(2,1)S(1)} all-to-all(bf16[16,2,96,384]{3,2,0,1:T(8,128)(2,1)S(1)} %copy.27), channel_id=1, replica_groups=mesh['pairs'=16,'core'=2,'fac'=4] {'core'}, dimensions={1} | all-to-all | bytes 4718592 | tf_op jit(solution)/shard_map/all_to_all | solution.py:47
  111.3 1.8 reduce_sum.137
  113.1 30.0 %all_to_all.45 = bf16[16,96,384]{2,1,0:T(8,128)(2,1)S(1)} all-to-all(bf16[16,96,384]{2,1,0:T(8,128)(2,1)} %reduce_sum.137), channel_id=1, replica_groups=mesh['pairs'=16,'core'=2,'fac'=4] {'pairs'}, dimensions={0} | all-to-all | bytes 2359296 | tf_op jit(solution)/shard_map/all_to_all | solution.py:49
  143.1 0.2 convert_reduce_fusion.2
  143.2 2.0 all-gather.7.cloned.1.call-done
  145.3 3.2 fusion.15
  148.5 11.5 %all_gather.23 = bf16[96,3072]{1,0:T(8,128)(2,1)S(1)} all-gather(bf16[96,768]{1,0:T(8,128)(2,1)S(1)} %fusion.15), channel_id=1, replica_groups=mesh['pairs'=16,'core'=2,'fac'=4] {'fac'}, dimensions={1}, use_global_device_ids=true | all-gather | bytes 737280 | tf_op jit(solution)/shard_map/all_gather | solution.py:79
  160.0 3.9 %fusion.27 = (bf16[96,768]{1,0:T(8,128)(2,1)}, f32[96,768]{1,0:T(8,128)S(1)}) fusion(bf16[96,3072]{1,0:T(8,128)(2,1)S(1)} %all_gather.23, bf16[3072,768]{1,0:T(8,128)(2,1)} %param.13), kind=kOutput, calls=%fused_computation.59 | convolution fusion | flops 453058560 | bytes 5750784 | tf_op jit(solution)/shard_map/dot_general | solution.py:78
  163.9 0.0 all-gather.11.cloned.1.call-start
  163.9 6.8 %fusion.4 = bf16[3072,384]{0,1:T(8,128)(2,1)} fusion(bf16[1024,3072]{1,0:T(8,128)(2,1)} %param.7, bf16[1024,768]{1,0:T(8,128)(2,1)S(1)} %copy-done.3), kind=kOutput, calls=%fused_computation.10 | convolution fusion | flops 2417098752 | bytes 9437184 | tf_op jit(solution)/shard_map/dot_general | solution.py:16
  170.8 3.0 copy.28
  173.8 0.2 copy.29
  174.0 7.5 %all_to_all.46 = bf16[16,2,96,384]{3,2,0,1:T(8,128)(2,1)S(1)} all-to-all(bf16[16,2,96,384]{3,2,0,1:T(8,128)(2,1)S(1)} %copy.29), channel_id=1, replica_groups=mesh['pairs'=16,'core'=2,'fac'=4] {'core'}, dimensions={1} | all-to-all | bytes 4718592 | tf_op jit(solution)/shard_map/all_to_all | solution.py:47
  181.5 1.8 reduce_sum.140
  183.3 26.3 %all_to_all.47 = bf16[16,96,384]{2,1,0:T(8,128)(2,1)S(1)} all-to-all(bf16[16,96,384]{2,1,0:T(8,128)(2,1)} %reduce_sum.140), channel_id=1, replica_groups=mesh['pairs'=16,'core'=2,'fac'=4] {'pairs'}, dimensions={0} | all-to-all | bytes 2359296 | tf_op jit(solution)/shard_map/all_to_all | solution.py:49
  209.6 0.2 convert_reduce_fusion.1
  209.8 11.7 %all_gather.24 = bf16[96,3072]{1,0:T(8,128)(2,1)S(1)} all-gather(bf16[96,768]{1,0:T(8,128)(2,1)S(1)} %pad_maximum_fusion), channel_id=1, replica_groups=mesh['pairs'=16,'core'=2,'fac'=4] {'fac'}, dimensions={1}, use_global_device_ids=true | all-gather | bytes 737280 | tf_op jit(solution)/shard_map/all_gather | solution.py:110
  221.5 4.5 %multiply_reduce_fusion.5 = (f32[]{:T(128)}, f32[]{:T(128)}, bf16[96,768]{1,0:T(8,128)(2,1)}, f32[96,768]{1,0:T(8,128)S(1)}) fusion(f32[96,768]{1,0:T(8,128)S(1)} %get-tuple-element.26, f32[96,768]{1,0:T(8,128)S(1)} %convert_reduce_fusion, bf16[96,3072]{1,0:T(8,128)(2,1)S(1)} %all_gather.24, bf16[3072,768]{1,0:T(8,128)(2,1)} %all-gather.9.cloned.1.call-done), kind=kOutput, calls=%fused_computation.43 | convolution fusion | flops 453574656 | bytes 6340616 | tf_op jit(solution)/shard_map/dot_general | solution.py:12
  226.0 0.0 all-gather.11.cloned.1.call-update
  226.0 3.3 convolution_convert_fusion.3
  229.3 1.4 pad_maximum_fusion.1
  230.6 0.7 broadcast_in_dim.7
  231.3 10.9 %all-to-all-start.6 = ((f32[128,1,2]{2,1,0:T(1,128)}), f32[128,1,2]{2,1,0:T(1,128)S(1)}, u32[]{:S(2)}, u32[]{:S(2)}) async-start(f32[128,1,2]{2,1,0:T(1,128)} %broadcast_in_dim.7), calls=%async_computation.6 | async-start | bytes 131072 | tf_op jit(solution)/shard_map/all_to_all | solution.py:56
  242.2 11.3 %all_gather.26 = bf16[96,3072]{1,0:T(8,128)(2,1)S(1)} all-gather(bf16[96,768]{1,0:T(8,128)(2,1)S(1)} %convolution_convert_fusion.3), channel_id=1, replica_groups=mesh['pairs'=16,'core'=2,'fac'=4] {'fac'}, dimensions={1}, use_global_device_ids=true | all-gather | bytes 737280 | tf_op jit(solution)/shard_map/all_gather | solution.py:119
  253.5 0.2 reduce_sum.143
  253.7 0.6 fusion.26
  255.7 20.6 %all-gather.11.cloned.1.call-done = bf16[3072,768]{1,0:T(8,128)(2,1)} async-done(((bf16[96,768]{1,0:T(8,128)(2,1)}), bf16[3072,768]{1,0:T(8,128)(2,1)}) %all-gather.11.cloned.1.call-update) | async-done | bytes 4718608 | tf_op jit(solution)/shard_map/all_gather | solution.py:73
  276.2 5.6 %fusion.6 = bf16[192,768]{1,0:T(8,128)(2,1)S(1)} fusion(bf16[3072,768]{1,0:T(8,128)(2,1)} %all-gather.11.cloned.1.call-done, bf16[3072,768]{1,0:T(8,128)(2,1)} %all-gather.7.cloned.1.call-done, f32[]{:T(128)S(6)} %div.17, bf16[96,3072]{1,0:T(8,128)(2,1)S(1)} %all_gather.26, bf16[96,3072]{1,0:T(8,128)(2,1)S(1)} %copy-done.5), kind=kOutput, calls=%fused_computation.18 | convolution fusion | flops 920272896 | bytes 10911748 | tf_op jit(solution)/shard_map/dot_general | solution.py:12
  281.8 1.3 collective-permute-start
  283.1 1.5 collective-permute-start.1
  284.6 1.7 fusion.13
  286.2 5.2 %collective-permute-done = bf16[192,768]{1,0:T(8,128)(2,1)S(1)} collective-permute-done((bf16[192,768]{1,0:T(8,128)(2,1)S(1)}, bf16[192,768]{1,0:T(8,128)(2,1)S(1)}, u32[]{:S(2)}, u32[]{:S(2)}) %collective-permute-start) | collective-permute-done | bytes 294944 | tf_op jit(solution)/shard_map/ppermute | solution.py:36
  291.4 1.7 convolution_add_fusion.2
  293.2 1.7 convolution_add_fusion.1
  294.9 5.2 %collective-permute-done.2 = bf16[192,768]{1,0:T(8,128)(2,1)S(1)} collective-permute-done((bf16[192,768]{1,0:T(8,128)(2,1)S(1)}, bf16[192,768]{1,0:T(8,128)(2,1)S(1)}, u32[]{:S(2)}, u32[]{:S(2)}) %collective-permute-start.2) | collective-permute-done | bytes 294944 | tf_op jit(solution)/shard_map/ppermute | solution.py:36
  300.1 1.7 convolution_add_fusion
  301.8 0.8 multiply_reduce_fusion.3
  302.6 2.5 pad_maximum_fusion.2
  305.2 16.0 %all_to_all.48 = f32[128,1,4]{2,1,0:T(1,128)S(1)} all-to-all(f32[128,1,4]{2,1,0:T(1,128)S(1)} %broadcast_in_dim.8), channel_id=1, replica_groups=mesh['pairs'=16,'core'=2,'fac'=4] {'pairs','core','fac'}, dimensions={0} | all-to-all | bytes 4096 | tf_op jit(solution)/shard_map/all_to_all | solution.py:56
  321.1 0.2 reduce_sum.148
  321.3 0.6 fusion.25
  326.4 1.0 multiply_subtract_fusion
  (24 shorter events, 0.1 us)
Async XLA Ops:
  7.2 78.7 %copy-start = (f32[32768]{0:T(1024)S(1)}, f32[32768]{0:T(1024)}, u32[]{:S(2)}) copy-start(f32[32768]{0:T(1024)} %param.11) | copy-start | bytes 393220
  7.2 77.9 %all-gather.5.cloned.1.call-start = ((), (), s32[]{:S(2)}) async-start(), calls=%async_computation.8 | async-start | bytes 4866048 | tf_op jit(solution)/shard_map/all_gather | solution.py:88
  8.8 136.4 %all-gather.7.cloned.1.call-start = ((), (), s32[]{:S(2)}) async-start(), calls=%async_computation.9 | async-start | bytes 4866048 | tf_op jit(solution)/shard_map/all_gather | solution.py:73
  41.5 44.3 %copy-start.7 = (s32[1024]{0:T(1024)S(1)}, s32[1024]{0:T(1024)}, u32[]{:S(2)}) copy-start(s32[1024]{0:T(1024)} %param.9) | copy-start | bytes 12292
  84.7 7.3 %copy-start.6 = (s32[1024]{0:T(1024)S(1)}, s32[1024]{0:T(1024)}, u32[]{:S(2)}) copy-start(s32[1024]{0:T(1024)} %param.10) | copy-start | bytes 12292
  85.8 135.7 %all-gather.9.cloned.1.call-start = ((), (), s32[]{:S(2)}) async-start(), calls=%async_computation.10 | async-start | bytes 4866048 | tf_op jit(solution)/shard_map/all_gather | solution.py:73
  93.8 1.1 copy-start.2
  111.3 34.0 %copy-start.4 = (bf16[96,3072]{1,0:T(8,128)(2,1)S(1)}, bf16[96,3072]{1,0:T(8,128)(2,1)}, u32[]{:S(2)}) copy-start(bf16[96,3072]{1,0:T(8,128)(2,1)} %param.12) | copy-start | bytes 1769476
  143.2 20.7 %copy-start.3 = (bf16[1024,768]{1,0:T(8,128)(2,1)S(1)}, bf16[1024,768]{1,0:T(8,128)(2,1)}, u32[]{:S(2)}) copy-start(bf16[1024,768]{1,0:T(8,128)(2,1)} %copy-done.2) | copy-start | bytes 4718596
  163.9 112.4 %all-gather.11.cloned.1.call-start = ((), (), s32[]{:S(2)}) async-start(), calls=%async_computation.11 | async-start | bytes 4866048 | tf_op jit(solution)/shard_map/all_gather | solution.py:73
  226.0 50.3 %copy-start.5 = (bf16[96,3072]{1,0:T(8,128)(2,1)S(1)}, bf16[96,3072]{1,0:T(8,128)(2,1)}, u32[]{:S(2)}) copy-start(bf16[96,3072]{1,0:T(8,128)(2,1)} %param.12) | copy-start | bytes 1769476
  231.3 22.2 %all-to-all-start.6 = ((f32[128,1,2]{2,1,0:T(1,128)}), f32[128,1,2]{2,1,0:T(1,128)S(1)}, u32[]{:S(2)}, u32[]{:S(2)}) async-start(f32[128,1,2]{2,1,0:T(1,128)} %broadcast_in_dim.7), calls=%async_computation.6 | async-start | bytes 131072 | tf_op jit(solution)/shard_map/all_to_all | solution.py:56
  281.8 9.6 %collective-permute-start = (bf16[192,768]{1,0:T(8,128)(2,1)S(1)}, bf16[192,768]{1,0:T(8,128)(2,1)S(1)}, u32[]{:S(2)}, u32[]{:S(2)}) collective-permute-start(bf16[192,768]{1,0:T(8,128)(2,1)S(1)} %fusion.6), channel_id=1, source_target_pairs={{0,1},{1,2},{2,3},{3,0},{4,5},{5,6},{6,7},{7,4},{8,9},{9,10},{10,1... | collective-permute-start | bytes 884744 | tf_op jit(solution)/shard_map/ppermute | solution.py:36
  283.1 10.1 %collective-permute-start.1 = (bf16[192,768]{1,0:T(8,128)(2,1)S(1)}, bf16[192,768]{1,0:T(8,128)(2,1)S(1)}, u32[]{:S(2)}, u32[]{:S(2)}) collective-permute-start(bf16[192,768]{1,0:T(8,128)(2,1)S(1)} %fusion.6), channel_id=1, source_target_pairs={{0,3},{1,0},{2,1},{3,2},{4,7},{5,4},{6,5},{7,6},{8,11},{9,8},{10,9... | collective-permute-start | bytes 884744 | tf_op jit(solution)/shard_map/ppermute | solution.py:39
  291.4 8.6 %collective-permute-start.2 = (bf16[192,768]{1,0:T(8,128)(2,1)S(1)}, bf16[192,768]{1,0:T(8,128)(2,1)S(1)}, u32[]{:S(2)}, u32[]{:S(2)}) collective-permute-start(bf16[192,768]{1,0:T(8,128)(2,1)S(1)} %collective-permute-done), channel_id=1, source_target_pairs={{0,1},{1,2},{2,3},{3,0},{4,5},{5,6},{6,7},{7,4},{8,9},{9,10},{10,1... | collective-permute-start | bytes 884744 | tf_op jit(solution)/shard_map/ppermute | solution.py:36
  291.4 35.9 %copy-start.1 = (f32[32768]{0:T(1024)S(1)}, f32[32768]{0:T(1024)}, u32[]{:S(2)}) copy-start(f32[32768]{0:T(1024)} %param.11) | copy-start | bytes 393220
Sparse Core Ops, SparseCore 0:
  10.8 68.8 all-gather.4
  85.9 59.2 all-gather.6
  164.0 53.3 all-gather.8
  226.1 50.0 all-gather.10
where the time goes:
time: 335 us; the launch traced here: 334 us
  blocking collectives  173 us (52%)
  matrix products  50.4 us (15%)
  waiting for transfers between devices  33.1 us (10%)
  local copies, waits for them, and re-layouts  26.6 us (8%)
  between operations  19.9 us (6%)
  other arithmetic  16.8 us (5%)
  starting transfers between devices  13.8 us (4%)
    all_to_all x3, blocking collectives, scatter_sum(): received = lax.all_to_all(chip_sum, 'pairs', 0, 0, tiled=False)  99.5 us
    all_to_all x3, blocking collectives, scatter_sum(): on_chip = lax.all_to_all(blocks, 'core', 1, 1, tiled=False)  23.4 us
    dot_general x8, matrix products, add_columns(): return jnp.dot(matrix, piece, preferred_element_type=jnp.float32)  23.3 us
    dot_general x3, matrix products, transposed_term(): lax.dot_general(matrix, right, (((0,), (0,)), ((), ())), preferred_elemen...  23.2 us
    all_gather x3, waiting for transfers between devices, gather_rows(): return lax.all_gather(matrix.astype(jnp.bfloat16), FSDP, axis=0, tiled=True)  22.6 us
    all_to_all x1, blocking collectives, global_sums(): received = lax.all_to_all(stacked, FSDP + ('fac',), 0, 0, tiled=True)  16 us
    all_gather x1, blocking collectives, body(): lax.all_gather(gram_own.astype(jnp.bfloat16), 'fac', axis=1, tiled=True)  11.7 us
    all_gather x1, blocking collectives, precondition(): lax.all_gather(mixed_low, 'fac', axis=1, tiled=True)  11.5 us
  transfers between devices with their start and end apart: 8, of which 4 were waited for; matrix products, arithmetic and copies ran while one was open for 20% of the time, Pallas kernels for 0%

commit v1 on v0

--- a/solution.py
+++ b/solution.py
@@ -6,6 +6,11 @@
 
 ITERS = 2
 damping = 0.3
+
+
+def gather_from_all(array, axis, dim):
+    copies = jnp.concatenate([array] * lax.axis_size(axis), axis=dim)
+    return lax.all_to_all(copies, axis, dim, dim, tiled=True)
 
 
 def add_columns(matrix, piece):
@@ -116,9 +121,7 @@
     image = curvature(direction)
     image_rows = gather_rows(image)
     inner_now, energy = global_sums(inner_part(residual, precond), inner_part(direction, image))
-    gram_inverse = lax.all_gather(
-        add_columns(gram_rows, in_cols).astype(jnp.bfloat16), "fac", axis=1, tiled=True
-    )
+    gram_inverse = gather_from_all(add_columns(gram_rows, in_cols).astype(jnp.bfloat16), "fac", 1)
     alpha = inner_now / energy
     newton_step = alpha * direction
     residual = residual - alpha * image

time: 335 us -> 336 us (level)
  blocking collectives: 173 us -> 162 us
  waiting for transfers between devices: 33.1 us -> 40 us
  starting transfers between devices: 13.8 us -> 17.4 us
    all_gather x1 -> x0, blocking collectives: 11.3 us -> none  [body(): lax.all_gather(add_columns(gram_rows, in_cols).astype(jnp.bfloat16), 'fac...]
    all_to_all x1, waiting for transfers between devices: 0.01 us -> 9.58 us  [global_sums(): received = lax.all_to_all(stacked, FSDP + ('fac',), 0, 0, tiled=True)]
    all_gather x3, waiting for transfers between devices: 22.6 us -> 13.9 us  [gather_rows(): return lax.all_gather(matrix.astype(jnp.bfloat16), FSDP, axis=0, tiled=True)]
    all_to_all x0 -> x1, waiting for transfers between devices: none -> 5.93 us  [gather_from_all(): return lax.all_to_all(copies, axis, dim, dim, tiled=True)]
    all_to_all x0 -> x1, starting transfers between devices: none -> 4.67 us  [gather_from_all(): return lax.all_to_all(copies, axis, dim, dim, tiled=True)]
  transfers between devices with their start and end apart: 8 -> 9, of which waited for: 4 -> 6; matrix products, arithmetic and copies ran while one was open for 20% -> 20% of each run, Pallas kernels for 0% -> 0%
where the time goes in v1:
time: 336 us; the launch traced here: 334 us
  blocking collectives  162 us (48%)
  matrix products  50.3 us (15%)
  waiting for transfers between devices  40 us (12%)
  local copies, waits for them, and re-layouts  27.5 us (8%)
  between operations  19.9 us (6%)
  starting transfers between devices  17.4 us (5%)
  other arithmetic  16.8 us (5%)
    all_to_all x3, blocking collectives, scatter_sum(): received = lax.all_to_all(chip_sum, 'pairs', 0, 0, tiled=False)  99.5 us
    all_to_all x3, blocking collectives, scatter_sum(): on_chip = lax.all_to_all(blocks, 'core', 1, 1, tiled=False)  23.4 us
    dot_general x8, matrix products, add_columns(): return jnp.dot(matrix, piece, preferred_element_type=jnp.float32)  23.2 us
    dot_general x3, matrix products, transposed_term(): lax.dot_general(matrix, right, (((0,), (0,)), ((), ())), preferred_elemen...  23.2 us
    all_to_all x1, blocking collectives, global_sums(): received = lax.all_to_all(stacked, FSDP + ('fac',), 0, 0, tiled=True)  15.9 us
    all_gather x3, waiting for transfers between devices, gather_rows(): return lax.all_gather(matrix.astype(jnp.bfloat16), FSDP, axis=0, tiled=True)  13.9 us
    all_gather x1, blocking collectives, body(): lax.all_gather(gram_own.astype(jnp.bfloat16), 'fac', axis=1, tiled=True)  11.7 us
    all_gather x1, blocking collectives, precondition(): lax.all_gather(mixed_low, 'fac', axis=1, tiled=True)  11.6 us
  transfers between devices with their start and end apart: 9, of which 6 were waited for; matrix products, arithmetic and copies ran while one was open for 20% of the time, Pallas kernels for 0%

profile of v1, /device:TPU:1, one launch (start us, length us, event | category | flops | bytes accessed | tf_op | source)
XLA Modules:
  0.0 334.0 jit_solution(7161897839390418423)
XLA Ops:
  7.2 0.0 all-gather.5.cloned.1.call-start
  7.2 1.6 constant_dynamic-slice_fusion
  8.8 0.0 all-gather.7.cloned.1.call-start
  8.9 0.7 convert_element_type.76
  9.6 9.4 %fusion.2 = bf16[3072,768]{0,1:T(8,128)(2,1)} fusion(bf16[1024,3072]{1,0:T(8,128)(2,1)} %param.7, bf16[1024,768]{1,0:T(8,128)(2,1)} %param.8, bf16[1024]{0:T(1024)(128)(2,1)S(1)} %convert_element_type.76), kind=kOutput, calls=%fused_computation.6 | convolution fusion | flops 4837343232 | bytes 12584960 | tf_op jit(solution)/shard_map/dot_general | solution.py:21
  19.0 6.7 %copy.35 = bf16[3072,768]{1,0:T(8,128)(2,1)} copy(bf16[3072,768]{0,1:T(8,128)(2,1)} %fusion.2) | data formatting | bytes 9437184 | tf_op jit(solution)/shard_map/convert_element_type | solution.py:74
  25.6 2.7 copy.36
  28.3 9.7 %all_to_all.54 = bf16[16,2,96,768]{3,2,0,1:T(8,128)(2,1)} all-to-all(bf16[16,2,96,768]{3,2,0,1:T(8,128)(2,1)S(1)} %copy.36), channel_id=1, replica_groups=mesh['pairs'=16,'core'=2,'fac'=4] {'core'}, dimensions={1} | all-to-all | bytes 9437184 | tf_op jit(solution)/shard_map/all_to_all | solution.py:52
  38.0 3.5 %reduce_sum.135 = bf16[16,96,768]{2,1,0:T(8,128)(2,1)S(1)} reduce(bf16[16,2,96,768]{3,2,0,1:T(8,128)(2,1)} %all_to_all.54, bf16[]{:T(256)} %constant.44.clone.1), dimensions={1}, to_apply=%region_0.0 | reduce | flops 1179648 | bytes 7077890 | tf_op jit(solution)/shard_map/reduce_sum | solution.py:53
  41.5 43.2 %all_to_all.55 = bf16[16,96,768]{2,1,0:T(8,128)(2,1)S(1)} all-to-all(bf16[16,96,768]{2,1,0:T(8,128)(2,1)S(1)} %reduce_sum.135), channel_id=1, replica_groups=mesh['pairs'=16,'core'=2,'fac'=4] {'pairs'}, dimensions={0} | all-to-all | bytes 4718592 | tf_op jit(solution)/shard_map/all_to_all | solution.py:54
  84.7 0.3 convert_reduce_fusion
  85.1 0.7 negate_convert_fusion
  85.8 0.0 all-gather.9.cloned.1.call-start
  85.9 6.2 %gather_fusion = f32[1024]{0:T(1024)S(1)} fusion(f32[32768]{0:T(1024)S(1)} %copy-done, s32[1024]{0:T(1024)S(1)} %fusion.19), kind=kCustom, calls=%fused_computation | custom fusion | bytes 12288 | tf_op jit(solution)/shard_map/gather | solution.py:70
  92.1 1.7 multiply_convert_fusion.1
  93.8 1.1 copy-done.2
  95.0 7.0 %fusion.3 = bf16[3072,384]{0,1:T(8,128)(2,1)} fusion(bf16[1024,3072]{1,0:T(8,128)(2,1)} %param.7, bf16[1024,768]{1,0:T(8,128)(2,1)S(1)} %multiply_convert_fusion.1), kind=kOutput, calls=%fused_computation.9 | convolution fusion | flops 2417098752 | bytes 9437184 | tf_op jit(solution)/shard_map/dot_general | solution.py:21
  101.9 3.0 copy.37
  104.9 0.2 copy.38
  105.2 6.1 %all_to_all.56 = bf16[16,2,96,384]{3,2,0,1:T(8,128)(2,1)S(1)} all-to-all(bf16[16,2,96,384]{3,2,0,1:T(8,128)(2,1)S(1)} %copy.38), channel_id=1, replica_groups=mesh['pairs'=16,'core'=2,'fac'=4] {'core'}, dimensions={1} | all-to-all | bytes 4718592 | tf_op jit(solution)/shard_map/all_to_all | solution.py:52
  111.3 1.8 reduce_sum.137
  113.1 30.0 %all_to_all.57 = bf16[16,96,384]{2,1,0:T(8,128)(2,1)S(1)} all-to-all(bf16[16,96,384]{2,1,0:T(8,128)(2,1)} %reduce_sum.137), channel_id=1, replica_groups=mesh['pairs'=16,'core'=2,'fac'=4] {'pairs'}, dimensions={0} | all-to-all | bytes 2359296 | tf_op jit(solution)/shard_map/all_to_all | solution.py:54
  143.1 0.2 convert_reduce_fusion.2
  143.2 2.0 all-gather.7.cloned.1.call-done
  145.3 3.2 fusion.15
  148.5 11.6 %all_gather.20 = bf16[96,3072]{1,0:T(8,128)(2,1)S(1)} all-gather(bf16[96,768]{1,0:T(8,128)(2,1)S(1)} %fusion.15), channel_id=1, replica_groups=mesh['pairs'=16,'core'=2,'fac'=4] {'fac'}, dimensions={1}, use_global_device_ids=true | all-gather | bytes 737280 | tf_op jit(solution)/shard_map/all_gather | solution.py:84
  160.1 3.9 %fusion.27 = (bf16[96,768]{1,0:T(8,128)(2,1)}, f32[96,768]{1,0:T(8,128)S(1)}) fusion(bf16[96,3072]{1,0:T(8,128)(2,1)S(1)} %all_gather.20, bf16[3072,768]{1,0:T(8,128)(2,1)} %param.13), kind=kOutput, calls=%fused_computation.61 | convolution fusion | flops 453058560 | bytes 5750784 | tf_op jit(solution)/shard_map/dot_general | solution.py:83
  164.0 0.0 all-gather.11.cloned.1.call-start
  164.1 6.8 %fusion.4 = bf16[3072,384]{0,1:T(8,128)(2,1)} fusion(bf16[1024,3072]{1,0:T(8,128)(2,1)} %param.7, bf16[1024,768]{1,0:T(8,128)(2,1)S(1)} %copy-done.3), kind=kOutput, calls=%fused_computation.10 | convolution fusion | flops 2417098752 | bytes 9437184 | tf_op jit(solution)/shard_map/dot_general | solution.py:21
  170.9 3.0 copy.39
  173.9 0.2 copy.40
  174.2 7.5 %all_to_all.58 = bf16[16,2,96,384]{3,2,0,1:T(8,128)(2,1)S(1)} all-to-all(bf16[16,2,96,384]{3,2,0,1:T(8,128)(2,1)S(1)} %copy.40), channel_id=1, replica_groups=mesh['pairs'=16,'core'=2,'fac'=4] {'core'}, dimensions={1} | all-to-all | bytes 4718592 | tf_op jit(solution)/shard_map/all_to_all | solution.py:52
  181.7 1.8 reduce_sum.140
  183.5 26.3 %all_to_all.59 = bf16[16,96,384]{2,1,0:T(8,128)(2,1)S(1)} all-to-all(bf16[16,96,384]{2,1,0:T(8,128)(2,1)} %reduce_sum.140), channel_id=1, replica_groups=mesh['pairs'=16,'core'=2,'fac'=4] {'pairs'}, dimensions={0} | all-to-all | bytes 2359296 | tf_op jit(solution)/shard_map/all_to_all | solution.py:54
  209.7 0.2 convert_reduce_fusion.1
  209.9 11.7 %all_gather.21 = bf16[96,3072]{1,0:T(8,128)(2,1)S(1)} all-gather(bf16[96,768]{1,0:T(8,128)(2,1)S(1)} %pad_maximum_fusion.1), channel_id=1, replica_groups=mesh['pairs'=16,'core'=2,'fac'=4] {'fac'}, dimensions={1}, use_global_device_ids=true | all-gather | bytes 737280 | tf_op jit(solution)/shard_map/all_gather | solution.py:115
  221.6 4.5 %multiply_reduce_fusion.5 = (f32[]{:T(128)}, f32[]{:T(128)}, bf16[96,768]{1,0:T(8,128)(2,1)}, f32[96,768]{1,0:T(8,128)S(1)}) fusion(f32[96,768]{1,0:T(8,128)S(1)} %get-tuple-element.26, f32[96,768]{1,0:T(8,128)S(1)} %convert_reduce_fusion, bf16[96,3072]{1,0:T(8,128)(2,1)S(1)} %all_gather.21, bf16[3072,768]{1,0:T(8,128)(2,1)} %all-gather.9.cloned.1.call-done), kind=kOutput, calls=%fused_computation.45 | convolution fusion | flops 453574656 | bytes 6340616 | tf_op jit(solution)/shard_map/dot_general | solution.py:17
  226.2 3.2 convolution_convert_fusion.3
  229.4 0.8 copy.56
  230.3 4.7 %all-to-all-start.7 = ((bf16[96,4,768]{2,0,1:T(8,128)(2,1)}), bf16[96,4,768]{2,0,1:T(8,128)(2,1)S(1)}, u32[]{:S(2)}, u32[]{:S(2)}) async-start(bf16[96,4,768]{2,0,1:T(8,128)(2,1)} %bitcast.42), calls=%async_computation.7 | async-start | bytes 1179648 | tf_op jit(solution)/shard_map/all_to_all | solution.py:13
  235.0 1.4 pad_maximum_fusion.2
  236.3 5.9 %all-to-all-done.7 = bf16[96,4,768]{2,0,1:T(8,128)(2,1)S(1)} async-done(((bf16[96,4,768]{2,0,1:T(8,128)(2,1)}), bf16[96,4,768]{2,0,1:T(8,128)(2,1)S(1)}, u32[]{:S(2)}, u32[]{:S(2)}) %all-to-all-start.7) | async-done | bytes 589856 | tf_op jit(solution)/shard_map/all_to_all | solution.py:13
  242.2 0.7 broadcast_in_dim.7
  242.9 9.8 %all-to-all-start.6 = ((f32[128,1,2]{2,1,0:T(1,128)}), f32[128,1,2]{2,1,0:T(1,128)S(1)}, u32[]{:S(2)}, u32[]{:S(2)}) async-start(f32[128,1,2]{2,1,0:T(1,128)} %broadcast_in_dim.7), calls=%async_computation.6 | async-start | bytes 131072 | tf_op jit(solution)/shard_map/all_to_all | solution.py:61
  252.7 0.1 copy.54
  252.8 9.6 %all-to-all-done.6 = f32[128,1,2]{2,1,0:T(1,128)S(1)} async-done(((f32[128,1,2]{2,1,0:T(1,128)}), f32[128,1,2]{2,1,0:T(1,128)S(1)}, u32[]{:S(2)}, u32[]{:S(2)}) %all-to-all-start.6) | async-done | bytes 1056 | tf_op jit(solution)/shard_map/all_to_all | solution.py:61
  262.4 0.2 reduce_sum.143
  262.5 0.6 fusion.26
  264.5 11.9 %all-gather.11.cloned.1.call-done = bf16[3072,768]{1,0:T(8,128)(2,1)} async-done(((bf16[96,768]{1,0:T(8,128)(2,1)}), bf16[3072,768]{1,0:T(8,128)(2,1)}) %all-gather.11.cloned.1.call-update) | async-done | bytes 4718608 | tf_op jit(solution)/shard_map/all_gather | solution.py:78
  276.4 5.6 %fusion.6 = bf16[192,768]{1,0:T(8,128)(2,1)S(1)} fusion(bf16[3072,768]{1,0:T(8,128)(2,1)} %all-gather.11.cloned.1.call-done, bf16[3072,768]{1,0:T(8,128)(2,1)} %all-gather.7.cloned.1.call-done, f32[]{:T(128)S(6)} %div.17, bf16[96,3072]{1,0:T(8,128)(2,1)S(1)} %bitcast.48, bf16[96,3072]{1,0:T(8,128)(2,1)S(1)} %copy-done.5), kind=kOutput, calls=%fused_computation.18 | convolution fusion | flops 920272896 | bytes 10911748 | tf_op jit(solution)/shard_map/dot_general | solution.py:17
  282.0 1.3 collective-permute-start
  283.2 1.5 collective-permute-start.1
  284.7 1.7 fusion.13
  286.4 5.2 %collective-permute-done = bf16[192,768]{1,0:T(8,128)(2,1)S(1)} collective-permute-done((bf16[192,768]{1,0:T(8,128)(2,1)S(1)}, bf16[192,768]{1,0:T(8,128)(2,1)S(1)}, u32[]{:S(2)}, u32[]{:S(2)}) %collective-permute-start) | collective-permute-done | bytes 294944 | tf_op jit(solution)/shard_map/ppermute | solution.py:41
  291.6 1.7 convolution_add_fusion.2
  293.3 1.7 convolution_add_fusion.1
  295.0 5.2 %collective-permute-done.2 = bf16[192,768]{1,0:T(8,128)(2,1)S(1)} collective-permute-done((bf16[192,768]{1,0:T(8,128)(2,1)S(1)}, bf16[192,768]{1,0:T(8,128)(2,1)S(1)}, u32[]{:S(2)}, u32[]{:S(2)}) %collective-permute-start.2) | collective-permute-done | bytes 294944 | tf_op jit(solution)/shard_map/ppermute | solution.py:41
  300.3 1.7 convolution_add_fusion
  301.9 0.8 multiply_reduce_fusion.3
  302.8 2.5 pad_maximum_fusion.3
  305.4 15.9 %all_to_all.60 = f32[128,1,4]{2,1,0:T(1,128)S(1)} all-to-all(f32[128,1,4]{2,1,0:T(1,128)S(1)} %broadcast_in_dim.8), channel_id=1, replica_groups=mesh['pairs'=16,'core'=2,'fac'=4] {'pairs','core','fac'}, dimensions={0} | all-to-all | bytes 4096 | tf_op jit(solution)/shard_map/all_to_all | solution.py:61
  321.3 0.2 reduce_sum.148
  321.4 0.6 fusion.25
  326.6 1.0 multiply_subtract_fusion
  (28 shorter events, 0.2 us)
Async XLA Ops:
  7.2 78.7 %copy-start = (f32[32768]{0:T(1024)S(1)}, f32[32768]{0:T(1024)}, u32[]{:S(2)}) copy-start(f32[32768]{0:T(1024)} %param.11) | copy-start | bytes 393220
  7.2 77.9 %all-gather.5.cloned.1.call-start = ((), (), s32[]{:S(2)}) async-start(), calls=%async_computation.9 | async-start | bytes 4866048 | tf_op jit(solution)/shard_map/all_gather | solution.py:93
  8.8 136.4 %all-gather.7.cloned.1.call-start = ((), (), s32[]{:S(2)}) async-start(), calls=%async_computation.10 | async-start | bytes 4866048 | tf_op jit(solution)/shard_map/all_gather | solution.py:78
  41.5 44.3 %copy-start.7 = (s32[1024]{0:T(1024)S(1)}, s32[1024]{0:T(1024)}, u32[]{:S(2)}) copy-start(s32[1024]{0:T(1024)} %param.9) | copy-start | bytes 12292
  84.7 7.3 %copy-start.6 = (s32[1024]{0:T(1024)S(1)}, s32[1024]{0:T(1024)}, u32[]{:S(2)}) copy-start(s32[1024]{0:T(1024)} %param.10) | copy-start | bytes 12292
  85.8 135.8 %all-gather.9.cloned.1.call-start = ((), (), s32[]{:S(2)}) async-start(), calls=%async_computation.11 | async-start | bytes 4866048 | tf_op jit(solution)/shard_map/all_gather | solution.py:78
  93.8 1.1 copy-start.2
  111.3 34.0 %copy-start.4 = (bf16[96,3072]{1,0:T(8,128)(2,1)S(1)}, bf16[96,3072]{1,0:T(8,128)(2,1)}, u32[]{:S(2)}) copy-start(bf16[96,3072]{1,0:T(8,128)(2,1)} %param.12) | copy-start | bytes 1769476
  148.5 15.6 %copy-start.3 = (bf16[1024,768]{1,0:T(8,128)(2,1)S(1)}, bf16[1024,768]{1,0:T(8,128)(2,1)}, u32[]{:S(2)}) copy-start(bf16[1024,768]{1,0:T(8,128)(2,1)} %copy-done.2) | copy-start | bytes 4718596
  164.0 112.4 %all-gather.11.cloned.1.call-start = ((), (), s32[]{:S(2)}) async-start(), calls=%async_computation.12 | async-start | bytes 4866048 | tf_op jit(solution)/shard_map/all_gather | solution.py:78
  229.4 47.0 %copy-start.5 = (bf16[96,3072]{1,0:T(8,128)(2,1)S(1)}, bf16[96,3072]{1,0:T(8,128)(2,1)}, u32[]{:S(2)}) copy-start(bf16[96,3072]{1,0:T(8,128)(2,1)} %param.12) | copy-start | bytes 1769476
  230.3 12.0 %all-to-all-start.7 = ((bf16[96,4,768]{2,0,1:T(8,128)(2,1)}), bf16[96,4,768]{2,0,1:T(8,128)(2,1)S(1)}, u32[]{:S(2)}, u32[]{:S(2)}) async-start(bf16[96,4,768]{2,0,1:T(8,128)(2,1)} %bitcast.42), calls=%async_computation.7 | async-start | bytes 1179648 | tf_op jit(solution)/shard_map/all_to_all | solution.py:13
  242.9 19.5 %all-to-all-start.6 = ((f32[128,1,2]{2,1,0:T(1,128)}), f32[128,1,2]{2,1,0:T(1,128)S(1)}, u32[]{:S(2)}, u32[]{:S(2)}) async-start(f32[128,1,2]{2,1,0:T(1,128)} %broadcast_in_dim.7), calls=%async_computation.6 | async-start | bytes 131072 | tf_op jit(solution)/shard_map/all_to_all | solution.py:61
  282.0 9.6 %collective-permute-start = (bf16[192,768]{1,0:T(8,128)(2,1)S(1)}, bf16[192,768]{1,0:T(8,128)(2,1)S(1)}, u32[]{:S(2)}, u32[]{:S(2)}) collective-permute-start(bf16[192,768]{1,0:T(8,128)(2,1)S(1)} %fusion.6), channel_id=1, source_target_pairs={{0,1},{1,2},{2,3},{3,0},{4,5},{5,6},{6,7},{7,4},{8,9},{9,10},{10,1... | collective-permute-start | bytes 884744 | tf_op jit(solution)/shard_map/ppermute | solution.py:41
  283.2 10.1 %collective-permute-start.1 = (bf16[192,768]{1,0:T(8,128)(2,1)S(1)}, bf16[192,768]{1,0:T(8,128)(2,1)S(1)}, u32[]{:S(2)}, u32[]{:S(2)}) collective-permute-start(bf16[192,768]{1,0:T(8,128)(2,1)S(1)} %fusion.6), channel_id=1, source_target_pairs={{0,3},{1,0},{2,1},{3,2},{4,7},{5,4},{6,5},{7,6},{8,11},{9,8},{10,9... | collective-permute-start | bytes 884744 | tf_op jit(solution)/shard_map/ppermute | solution.py:44
  291.6 8.6 %collective-permute-start.2 = (bf16[192,768]{1,0:T(8,128)(2,1)S(1)}, bf16[192,768]{1,0:T(8,128)(2,1)S(1)}, u32[]{:S(2)}, u32[]{:S(2)}) collective-permute-start(bf16[192,768]{1,0:T(8,128)(2,1)S(1)} %collective-permute-done), channel_id=1, source_target_pairs={{0,1},{1,2},{2,3},{3,0},{4,5},{5,6},{6,7},{7,4},{8,9},{9,10},{10,1... | collective-permute-start | bytes 884744 | tf_op jit(solution)/shard_map/ppermute | solution.py:41
  293.3 34.2 %copy-start.1 = (f32[32768]{0:T(1024)S(1)}, f32[32768]{0:T(1024)}, u32[]{:S(2)}) copy-start(f32[32768]{0:T(1024)} %param.11) | copy-start | bytes 393220
Sparse Core Ops, SparseCore 0:
  10.8 68.8 all-gather.4
  85.9 59.2 all-gather.6
  164.1 53.3 all-gather.8
  226.3 50.0 all-gather.10
